TPU v7x, 256 devices: a whole 4x4x8 slice. The times are simulated.
256 devices in a mesh: dp: 16 (over x, y_lo, core), expert: 16 (over z, y_hi).
Axes of the slice: x: 4, y: 4 (y_hi: 2, y_lo: 2; y = y_hi * 2 + y_lo), z: 8, core: 2. Of those that a mesh axis runs over, the one named last changes fastest.
Arguments:
- tokens: bfloat16 [32768, 2048], P(('dp', 'expert')), may hold values from -6 to 6
- gain: float32 [2048], replicated, may hold values from 0.1 to 1.9
- expert_ids: int32 [32768, 8], P(('dp', 'expert')), may hold values from 0 to 15, all different within a row; in each aligned block of 128 rows (0 to 127, 128 to 255, ...) at most 96 rows name the same one
- gate_values: float32 [32768, 8], P(('dp', 'expert')), may hold values from 0.02 to 0.25
- w_gate: bfloat16 [16, 2048, 768], P('expert'), may hold values from -0.125 to 0.125
- w_up: bfloat16 [16, 2048, 768], P('expert'), may hold values from -0.125 to 0.125
- w_down: bfloat16 [16, 768, 2048], P('expert'), may hold values from -0.21875 to 0.21875
Outputs:
- mixed: bfloat16 [32768, 2048], P(('dp', 'expert'))
Inputs may be any that keep to these rules, and one draw needn't show every extreme that they name: `expert_ids`: each row names 8 different experts. In the rows of one device no expert is named by more than 96 rows, and in every draw some expert is named by exactly 96 rows of some device.
All inputs are finite; a program needn't handle non-finite values.
Results may differ from a plain program's by a relative error of at most 0.018.
Values may be sent and summed in bfloat16 or wider, within the bound.
No kernel may reach another device: no remote copies, remote signals or barrier semaphores. Data moves between devices by JAX's collectives and lax.ppermute only.
A program may use at most 128 MiB of HBM per device.

v0:
```python
import jax
import jax.numpy as jnp
from jax import lax
from jax.sharding import PartitionSpec as P

eps_value = 1e-06


def passed_along(block, axis, distance):
    devices = range(lax.axis_size(axis))
    route = [((i - distance) % len(devices), i) for i in devices]
    return lax.ppermute(block, axis, route)


def normalize(tokens, gain):
    values = tokens.astype(jnp.float32)
    meansq = jnp.mean(values * values, axis=-1, keepdims=True)
    return (values * lax.rsqrt(meansq + eps_value) * gain).astype(jnp.bfloat16)


def gate_dense(expert_ids, gate_values, number):
    labels = jnp.arange(number, dtype=jnp.int32)
    hits = (expert_ids[..., None] == labels).astype(jnp.float32)
    return jnp.sum(hits * gate_values[..., None], axis=-2)


def dispatch_table(column, capacity):
    matched = (column > 0).astype(jnp.float32)
    slots = jnp.cumsum(matched, axis=-1) - 1.0
    places = jnp.arange(capacity).astype(jnp.float32)
    chosen = (slots[..., None, :] == places[:, None]) & (matched[..., None, :] > 0)
    return chosen.astype(jnp.bfloat16)


def expert_mlp(slot_rows, gate_matrix, up_matrix, down_matrix):
    gated = jnp.dot(slot_rows, gate_matrix, preferred_element_type=jnp.float32)
    upward = jnp.dot(slot_rows, up_matrix, preferred_element_type=jnp.float32)
    hidden = (jax.nn.silu(gated) * upward).astype(jnp.bfloat16)
    return jnp.dot(hidden, down_matrix, preferred_element_type=jnp.float32).astype(jnp.bfloat16)


def place_block(buffer, table, carried, source):
    picked = lax.dynamic_index_in_dim(table, source, 0, keepdims=False)
    slot_rows = jnp.dot(picked, carried, preferred_element_type=jnp.float32).astype(jnp.bfloat16)
    return lax.dynamic_update_index_in_dim(buffer, slot_rows, source, 0)


def local(tokens, gain, expert_ids, gate_values, w_gate, w_up, w_down):
    group = lax.axis_size("expert")
    position = lax.axis_index("expert")
    local_rows = tokens.shape[0]
    width = tokens.shape[1]
    chosen_count = expert_ids.shape[1]
    capacity = local_rows * chosen_count // group * 3 // 2
    gate_matrix = w_gate[0]
    up_matrix = w_up[0]
    down_matrix = w_down[0]
    normed = normalize(tokens, gain)
    dense = gate_dense(expert_ids, gate_values, group)
    gathered = lax.all_gather(dense, "expert", axis=0, tiled=True)
    column = lax.dynamic_slice_in_dim(gathered, position, 1, 1).reshape(group, local_rows)
    table = dispatch_table(column, capacity)
    buffer = jnp.zeros((group, capacity, width), jnp.bfloat16)
    buffer = place_block(buffer, table, normed, position)

    def forward_turn(offset, state):
        current, carried = state
        carried = passed_along(carried, "expert", 1)
        source = (position - offset) % group
        return (place_block(current, table, carried, source), carried)

    buffer, carried = lax.fori_loop(1, group, forward_turn, (buffer, normed))
    outputs = expert_mlp(
        buffer.reshape(group * capacity, width), gate_matrix, up_matrix, down_matrix
    )
    outputs = outputs.reshape(group, capacity, width)
    spanned = local_rows * lax.axis_size("expert") // local_rows
    back = jnp.einsum("bct,bcd->btd", table, outputs, preferred_element_type=jnp.float32)
    return lax.psum_scatter(
        (back * column[:, :, None]).reshape(spanned * local_rows, width).astype(jnp.bfloat16),
        "expert",
        scatter_dimension=0,
        tiled=True,
    )


def solution(mesh):
    return jax.shard_map(
        local,
        mesh=mesh,
        in_specs=(
            P(("dp", "expert"), None),
            P(),
            P(("dp", "expert"), None),
            P(("dp", "expert"), None),
            P("expert", None, None),
            P("expert", None, None),
            P("expert", None, None),
        ),
        out_specs=P(("dp", "expert"), None),
        check_vma=False,
    )
```

profile of v0, /device:TPU:2, one launch (start us, length us, event | category | flops | bytes accessed | tf_op | source)
XLA Modules:
  0.0 603.0 jit_solution(9800306333503433712)
XLA Ops:
  9.3 44.7 %all_gather.3 = f32[2048,16]{0,1:T(8,128)S(1)} all-gather(f32[128,16]{0,1:T(8,128)S(1)} %select_reduce_fusion), channel_id=1, replica_groups=mesh['dp'=16,'expert'=16] {'expert'}, dimensions={0}, use_global_device_ids=true | all-gather | bytes 139264 | tf_op jit(solution)/shard_map/all_gather | solution.py:60
  58.2 2.6 copy-done.1
  60.8 287.0 %while.17 = (s32[]{:T(128)}, bf16[16,96,2048]{2,1,0:T(8,128)(2,1)}, bf16[128,2048]{1,0:T(8,128)(2,1)}, s32[]{:T(128)}, bf16[16,96,128]{2,1,0:T(8,128)(2,1)S(1)},...) while((s32[]{:T(128)}, bf16[16,96,2048]{2,1,0:T(8,128)(2,1)}, bf16[128,2048]{1,0:T(8,128)(2,1)}, s32[]{:T(128)}, ...), condition=%wide.region_4.5_spmd, body=%wide.region_3.4_spmd.sunk | while | flops 50528272 | bytes 4089120 | solution.py:72
  60.8 13.1 %collective-permute-done = bf16[128,2048]{1,0:T(8,128)(2,1)} collective-permute-done((bf16[128,2048]{1,0:T(8,128)(2,1)}, bf16[128,2048]{1,0:T(8,128)(2,1)}, u32[]{:S(2)}, u32[]{:S(2)}) %collective-permute-start) | collective-permute-done | bytes 524320 | tf_op jit(solution)/shard_map/while/body/eval_jaxpr/ppermute | solution.py:12
  75.8 2.1 fusion.29
  77.8 13.1 %collective-permute-done = bf16[128,2048]{1,0:T(8,128)(2,1)} collective-permute-done((bf16[128,2048]{1,0:T(8,128)(2,1)}, bf16[128,2048]{1,0:T(8,128)(2,1)}, u32[]{:S(2)}, u32[]{:S(2)}) %collective-permute-start) | collective-permute-done | bytes 524320 | tf_op jit(solution)/shard_map/while/body/eval_jaxpr/ppermute | solution.py:12
  92.8 2.1 fusion.29
  94.9 13.5 %collective-permute-done = bf16[128,2048]{1,0:T(8,128)(2,1)} collective-permute-done((bf16[128,2048]{1,0:T(8,128)(2,1)}, bf16[128,2048]{1,0:T(8,128)(2,1)}, u32[]{:S(2)}, u32[]{:S(2)}) %collective-permute-start) | collective-permute-done | bytes 524320 | tf_op jit(solution)/shard_map/while/body/eval_jaxpr/ppermute | solution.py:12
  110.3 2.1 fusion.29
  112.4 14.6 %collective-permute-done = bf16[128,2048]{1,0:T(8,128)(2,1)} collective-permute-done((bf16[128,2048]{1,0:T(8,128)(2,1)}, bf16[128,2048]{1,0:T(8,128)(2,1)}, u32[]{:S(2)}, u32[]{:S(2)}) %collective-permute-start) | collective-permute-done | bytes 524320 | tf_op jit(solution)/shard_map/while/body/eval_jaxpr/ppermute | solution.py:12
  128.9 2.1 fusion.29
  131.0 15.8 %collective-permute-done = bf16[128,2048]{1,0:T(8,128)(2,1)} collective-permute-done((bf16[128,2048]{1,0:T(8,128)(2,1)}, bf16[128,2048]{1,0:T(8,128)(2,1)}, u32[]{:S(2)}, u32[]{:S(2)}) %collective-permute-start) | collective-permute-done | bytes 524320 | tf_op jit(solution)/shard_map/while/body/eval_jaxpr/ppermute | solution.py:12
  148.6 2.0 fusion.29
  150.7 16.9 %collective-permute-done = bf16[128,2048]{1,0:T(8,128)(2,1)} collective-permute-done((bf16[128,2048]{1,0:T(8,128)(2,1)}, bf16[128,2048]{1,0:T(8,128)(2,1)}, u32[]{:S(2)}, u32[]{:S(2)}) %collective-permute-start) | collective-permute-done | bytes 524320 | tf_op jit(solution)/shard_map/while/body/eval_jaxpr/ppermute | solution.py:12
  171.6 18.1 %collective-permute-done = bf16[128,2048]{1,0:T(8,128)(2,1)} collective-permute-done((bf16[128,2048]{1,0:T(8,128)(2,1)}, bf16[128,2048]{1,0:T(8,128)(2,1)}, u32[]{:S(2)}, u32[]{:S(2)}) %collective-permute-start) | collective-permute-done | bytes 524320 | tf_op jit(solution)/shard_map/while/body/eval_jaxpr/ppermute | solution.py:12
  193.6 18.2 %collective-permute-done = bf16[128,2048]{1,0:T(8,128)(2,1)} collective-permute-done((bf16[128,2048]{1,0:T(8,128)(2,1)}, bf16[128,2048]{1,0:T(8,128)(2,1)}, u32[]{:S(2)}, u32[]{:S(2)}) %collective-permute-start) | collective-permute-done | bytes 524320 | tf_op jit(solution)/shard_map/while/body/eval_jaxpr/ppermute | solution.py:12
  215.7 17.4 %collective-permute-done = bf16[128,2048]{1,0:T(8,128)(2,1)} collective-permute-done((bf16[128,2048]{1,0:T(8,128)(2,1)}, bf16[128,2048]{1,0:T(8,128)(2,1)}, u32[]{:S(2)}, u32[]{:S(2)}) %collective-permute-start) | collective-permute-done | bytes 524320 | tf_op jit(solution)/shard_map/while/body/eval_jaxpr/ppermute | solution.py:12
  235.0 2.1 fusion.29
  237.0 16.5 %collective-permute-done = bf16[128,2048]{1,0:T(8,128)(2,1)} collective-permute-done((bf16[128,2048]{1,0:T(8,128)(2,1)}, bf16[128,2048]{1,0:T(8,128)(2,1)}, u32[]{:S(2)}, u32[]{:S(2)}) %collective-permute-start) | collective-permute-done | bytes 524320 | tf_op jit(solution)/shard_map/while/body/eval_jaxpr/ppermute | solution.py:12
  257.4 15.7 %collective-permute-done = bf16[128,2048]{1,0:T(8,128)(2,1)} collective-permute-done((bf16[128,2048]{1,0:T(8,128)(2,1)}, bf16[128,2048]{1,0:T(8,128)(2,1)}, u32[]{:S(2)}, u32[]{:S(2)}) %collective-permute-start) | collective-permute-done | bytes 524320 | tf_op jit(solution)/shard_map/while/body/eval_jaxpr/ppermute | solution.py:12
  275.0 2.1 fusion.29
  277.1 14.8 %collective-permute-done = bf16[128,2048]{1,0:T(8,128)(2,1)} collective-permute-done((bf16[128,2048]{1,0:T(8,128)(2,1)}, bf16[128,2048]{1,0:T(8,128)(2,1)}, u32[]{:S(2)}, u32[]{:S(2)}) %collective-permute-start) | collective-permute-done | bytes 524320 | tf_op jit(solution)/shard_map/while/body/eval_jaxpr/ppermute | solution.py:12
  293.7 2.1 fusion.29
  295.8 13.9 %collective-permute-done = bf16[128,2048]{1,0:T(8,128)(2,1)} collective-permute-done((bf16[128,2048]{1,0:T(8,128)(2,1)}, bf16[128,2048]{1,0:T(8,128)(2,1)}, u32[]{:S(2)}, u32[]{:S(2)}) %collective-permute-start) | collective-permute-done | bytes 524320 | tf_op jit(solution)/shard_map/while/body/eval_jaxpr/ppermute | solution.py:12
  311.6 2.1 fusion.29
  313.7 13.1 %collective-permute-done = bf16[128,2048]{1,0:T(8,128)(2,1)} collective-permute-done((bf16[128,2048]{1,0:T(8,128)(2,1)}, bf16[128,2048]{1,0:T(8,128)(2,1)}, u32[]{:S(2)}, u32[]{:S(2)}) %collective-permute-start) | collective-permute-done | bytes 524320 | tf_op jit(solution)/shard_map/while/body/eval_jaxpr/ppermute | solution.py:12
  330.7 13.1 %collective-permute-done = bf16[128,2048]{1,0:T(8,128)(2,1)} collective-permute-done((bf16[128,2048]{1,0:T(8,128)(2,1)}, bf16[128,2048]{1,0:T(8,128)(2,1)}, u32[]{:S(2)}, u32[]{:S(2)}) %collective-permute-start) | collective-permute-done | bytes 524320 | tf_op jit(solution)/shard_map/while/body/eval_jaxpr/ppermute | solution.py:12
  347.8 8.2 %fusion.7 = f32[1536,768]{1,0:T(8,128)S(1)} fusion(bf16[1536,2048]{1,0:T(8,128)(2,1)} %bitcast.40, bf16[1,2048,768]{2,1,0:T(8,128)(2,1)} %param.13), kind=kOutput, calls=%fused_computation.11 | convolution fusion | flops 4831838208 | bytes 14155776 | tf_op jit(solution)/shard_map/dot_general | solution.py:36
  356.0 5.6 multiply_convert_fusion.1
  361.6 5.3 convolution_convert_fusion.1
  367.0 4.8 multiply_convert_fusion
  371.7 224.4 %reduce-scatter.2.cloned.1.call-done = bf16[128,2048]{1,0:T(8,128)(2,1)} async-done(((bf16[2048,2048]{1,0:T(8,128)(2,1)}), bf16[128,2048]{1,0:T(8,128)(2,1)}) %reduce-scatter.2.cloned.1.call-update) | async-done | bytes 524304 | tf_op jit(solution)/shard_map/reduce_scatter | solution.py:79
  (63 shorter events, 47.4 us)
Async XLA Ops:
  6.5 355.1 %copy-start = (bf16[1,768,2048]{2,1,0:T(8,128)(2,1)S(1)}, bf16[1,768,2048]{2,1,0:T(8,128)(2,1)}, u32[]{:S(2)}) copy-start(bf16[1,768,2048]{2,1,0:T(8,128)(2,1)} %param.15) | copy-start | bytes 9437188
  6.5 589.6 %reduce-scatter.2.cloned.1.call-start = ((), (), s32[]{:S(2)}) async-start(), calls=%async_computation.1 | async-start | bytes 8912896 | tf_op jit(solution)/shard_map/reduce_scatter | solution.py:79
  56.1 2.0 copy-start.3
  58.1 2.6 copy-start.1
  60.8 13.1 %collective-permute-start = (bf16[128,2048]{1,0:T(8,128)(2,1)}, bf16[128,2048]{1,0:T(8,128)(2,1)}, u32[]{:S(2)}, u32[]{:S(2)}) collective-permute-start(bf16[128,2048]{1,0:T(8,128)(2,1)} %get-tuple-element.195), channel_id=1, source_target_pairs={{15,0},{0,1},{1,2},{2,3},{3,4},{4,5},{5,6},{6,7},{7,8},{8,9},{9,10... | collective-permute-start | bytes 1572872 | tf_op jit(solution)/shard_map/while/body/eval_jaxpr/ppermute | solution.py:12
  77.8 13.1 %collective-permute-start = (bf16[128,2048]{1,0:T(8,128)(2,1)}, bf16[128,2048]{1,0:T(8,128)(2,1)}, u32[]{:S(2)}, u32[]{:S(2)}) collective-permute-start(bf16[128,2048]{1,0:T(8,128)(2,1)} %get-tuple-element.195), channel_id=1, source_target_pairs={{15,0},{0,1},{1,2},{2,3},{3,4},{4,5},{5,6},{6,7},{7,8},{8,9},{9,10... | collective-permute-start | bytes 1572872 | tf_op jit(solution)/shard_map/while/body/eval_jaxpr/ppermute | solution.py:12
  94.9 13.5 %collective-permute-start = (bf16[128,2048]{1,0:T(8,128)(2,1)}, bf16[128,2048]{1,0:T(8,128)(2,1)}, u32[]{:S(2)}, u32[]{:S(2)}) collective-permute-start(bf16[128,2048]{1,0:T(8,128)(2,1)} %get-tuple-element.195), channel_id=1, source_target_pairs={{15,0},{0,1},{1,2},{2,3},{3,4},{4,5},{5,6},{6,7},{7,8},{8,9},{9,10... | collective-permute-start | bytes 1572872 | tf_op jit(solution)/shard_map/while/body/eval_jaxpr/ppermute | solution.py:12
  112.4 14.7 %collective-permute-start = (bf16[128,2048]{1,0:T(8,128)(2,1)}, bf16[128,2048]{1,0:T(8,128)(2,1)}, u32[]{:S(2)}, u32[]{:S(2)}) collective-permute-start(bf16[128,2048]{1,0:T(8,128)(2,1)} %get-tuple-element.195), channel_id=1, source_target_pairs={{15,0},{0,1},{1,2},{2,3},{3,4},{4,5},{5,6},{6,7},{7,8},{8,9},{9,10... | collective-permute-start | bytes 1572872 | tf_op jit(solution)/shard_map/while/body/eval_jaxpr/ppermute | solution.py:12
  131.0 15.8 %collective-permute-start = (bf16[128,2048]{1,0:T(8,128)(2,1)}, bf16[128,2048]{1,0:T(8,128)(2,1)}, u32[]{:S(2)}, u32[]{:S(2)}) collective-permute-start(bf16[128,2048]{1,0:T(8,128)(2,1)} %get-tuple-element.195), channel_id=1, source_target_pairs={{15,0},{0,1},{1,2},{2,3},{3,4},{4,5},{5,6},{6,7},{7,8},{8,9},{9,10... | collective-permute-start | bytes 1572872 | tf_op jit(solution)/shard_map/while/body/eval_jaxpr/ppermute | solution.py:12
  150.7 17.0 %collective-permute-start = (bf16[128,2048]{1,0:T(8,128)(2,1)}, bf16[128,2048]{1,0:T(8,128)(2,1)}, u32[]{:S(2)}, u32[]{:S(2)}) collective-permute-start(bf16[128,2048]{1,0:T(8,128)(2,1)} %get-tuple-element.195), channel_id=1, source_target_pairs={{15,0},{0,1},{1,2},{2,3},{3,4},{4,5},{5,6},{6,7},{7,8},{8,9},{9,10... | collective-permute-start | bytes 1572872 | tf_op jit(solution)/shard_map/while/body/eval_jaxpr/ppermute | solution.py:12
  171.6 18.1 %collective-permute-start = (bf16[128,2048]{1,0:T(8,128)(2,1)}, bf16[128,2048]{1,0:T(8,128)(2,1)}, u32[]{:S(2)}, u32[]{:S(2)}) collective-permute-start(bf16[128,2048]{1,0:T(8,128)(2,1)} %get-tuple-element.195), channel_id=1, source_target_pairs={{15,0},{0,1},{1,2},{2,3},{3,4},{4,5},{5,6},{6,7},{7,8},{8,9},{9,10... | collective-permute-start | bytes 1572872 | tf_op jit(solution)/shard_map/while/body/eval_jaxpr/ppermute | solution.py:12
  193.6 18.2 %collective-permute-start = (bf16[128,2048]{1,0:T(8,128)(2,1)}, bf16[128,2048]{1,0:T(8,128)(2,1)}, u32[]{:S(2)}, u32[]{:S(2)}) collective-permute-start(bf16[128,2048]{1,0:T(8,128)(2,1)} %get-tuple-element.195), channel_id=1, source_target_pairs={{15,0},{0,1},{1,2},{2,3},{3,4},{4,5},{5,6},{6,7},{7,8},{8,9},{9,10... | collective-permute-start | bytes 1572872 | tf_op jit(solution)/shard_map/while/body/eval_jaxpr/ppermute | solution.py:12
  215.7 17.4 %collective-permute-start = (bf16[128,2048]{1,0:T(8,128)(2,1)}, bf16[128,2048]{1,0:T(8,128)(2,1)}, u32[]{:S(2)}, u32[]{:S(2)}) collective-permute-start(bf16[128,2048]{1,0:T(8,128)(2,1)} %get-tuple-element.195), channel_id=1, source_target_pairs={{15,0},{0,1},{1,2},{2,3},{3,4},{4,5},{5,6},{6,7},{7,8},{8,9},{9,10... | collective-permute-start | bytes 1572872 | tf_op jit(solution)/shard_map/while/body/eval_jaxpr/ppermute | solution.py:12
  237.0 16.5 %collective-permute-start = (bf16[128,2048]{1,0:T(8,128)(2,1)}, bf16[128,2048]{1,0:T(8,128)(2,1)}, u32[]{:S(2)}, u32[]{:S(2)}) collective-permute-start(bf16[128,2048]{1,0:T(8,128)(2,1)} %get-tuple-element.195), channel_id=1, source_target_pairs={{15,0},{0,1},{1,2},{2,3},{3,4},{4,5},{5,6},{6,7},{7,8},{8,9},{9,10... | collective-permute-start | bytes 1572872 | tf_op jit(solution)/shard_map/while/body/eval_jaxpr/ppermute | solution.py:12
  257.4 15.7 %collective-permute-start = (bf16[128,2048]{1,0:T(8,128)(2,1)}, bf16[128,2048]{1,0:T(8,128)(2,1)}, u32[]{:S(2)}, u32[]{:S(2)}) collective-permute-start(bf16[128,2048]{1,0:T(8,128)(2,1)} %get-tuple-element.195), channel_id=1, source_target_pairs={{15,0},{0,1},{1,2},{2,3},{3,4},{4,5},{5,6},{6,7},{7,8},{8,9},{9,10... | collective-permute-start | bytes 1572872 | tf_op jit(solution)/shard_map/while/body/eval_jaxpr/ppermute | solution.py:12
  277.1 14.8 %collective-permute-start = (bf16[128,2048]{1,0:T(8,128)(2,1)}, bf16[128,2048]{1,0:T(8,128)(2,1)}, u32[]{:S(2)}, u32[]{:S(2)}) collective-permute-start(bf16[128,2048]{1,0:T(8,128)(2,1)} %get-tuple-element.195), channel_id=1, source_target_pairs={{15,0},{0,1},{1,2},{2,3},{3,4},{4,5},{5,6},{6,7},{7,8},{8,9},{9,10... | collective-permute-start | bytes 1572872 | tf_op jit(solution)/shard_map/while/body/eval_jaxpr/ppermute | solution.py:12
  295.8 13.9 %collective-permute-start = (bf16[128,2048]{1,0:T(8,128)(2,1)}, bf16[128,2048]{1,0:T(8,128)(2,1)}, u32[]{:S(2)}, u32[]{:S(2)}) collective-permute-start(bf16[128,2048]{1,0:T(8,128)(2,1)} %get-tuple-element.195), channel_id=1, source_target_pairs={{15,0},{0,1},{1,2},{2,3},{3,4},{4,5},{5,6},{6,7},{7,8},{8,9},{9,10... | collective-permute-start | bytes 1572872 | tf_op jit(solution)/shard_map/while/body/eval_jaxpr/ppermute | solution.py:12
  313.7 13.1 %collective-permute-start = (bf16[128,2048]{1,0:T(8,128)(2,1)}, bf16[128,2048]{1,0:T(8,128)(2,1)}, u32[]{:S(2)}, u32[]{:S(2)}) collective-permute-start(bf16[128,2048]{1,0:T(8,128)(2,1)} %get-tuple-element.195), channel_id=1, source_target_pairs={{15,0},{0,1},{1,2},{2,3},{3,4},{4,5},{5,6},{6,7},{7,8},{8,9},{9,10... | collective-permute-start | bytes 1572872 | tf_op jit(solution)/shard_map/while/body/eval_jaxpr/ppermute | solution.py:12
  330.7 13.1 %collective-permute-start = (bf16[128,2048]{1,0:T(8,128)(2,1)}, bf16[128,2048]{1,0:T(8,128)(2,1)}, u32[]{:S(2)}, u32[]{:S(2)}) collective-permute-start(bf16[128,2048]{1,0:T(8,128)(2,1)} %get-tuple-element.195), channel_id=1, source_target_pairs={{15,0},{0,1},{1,2},{2,3},{3,4},{4,5},{5,6},{6,7},{7,8},{8,9},{9,10... | collective-permute-start | bytes 1572872 | tf_op jit(solution)/shard_map/while/body/eval_jaxpr/ppermute | solution.py:12
  347.8 8.2 %copy-start.2 = (bf16[16,96,2048]{2,1,0:T(8,128)(2,1)S(1)}, bf16[16,96,2048]{2,1,0:T(8,128)(2,1)}, u32[]{:S(2)}) copy-start(bf16[16,96,2048]{2,1,0:T(8,128)(2,1)} %get-tuple-element.138) | copy-start | bytes 18874372
  347.8 8.2 %copy-start.6 = (bf16[1,2048,768]{2,1,0:T(8,128)(2,1)S(1)}, bf16[1,2048,768]{2,1,0:T(8,128)(2,1)}, u32[]{:S(2)}) copy-start(bf16[1,2048,768]{2,1,0:T(8,128)(2,1)} %param.14) | copy-start | bytes 9437188
  361.6 5.3 copy-start.4
  361.6 5.3 copy-start.5
Sparse Core Ops, SparseCore 0:
  371.9 224.2 reduce-scatter.1
where the time goes:
time: 605 us; the launch traced here: 603 us
  waiting for transfers between devices  452 us (75%)
  matrix products  55 us (9%)
  blocking collectives  44.7 us (7%)
  local copies, waits for them, and re-layouts  31.7 us (5%)
  between operations  13.5 us (2%)
    ppermute x15, waiting for transfers between devices, passed_along(): return lax.ppermute(block, axis, route)  228 us
    reduce_scatter x1, waiting for transfers between devices, local(): lax.psum_scatter((back * column[:, :, None]).reshape(spanned * local_rows...  224 us
    all_gather x1, blocking collectives, local(): gathered = lax.all_gather(dense, 'expert', axis=0, tiled=True)  44.7 us
    dot_general x16, matrix products, place_block(): jnp.dot(picked, carried, preferred_element_type=jnp.float32)  31.1 us
    while x15, local copies, waits for them, and re-layouts  28.2 us
  transfers between devices with their start and end apart: 16, of which 16 were waited for; matrix products, arithmetic and copies ran while one was open for 0% of the time, Pallas kernels for 0%

commit v1 on v0

v1 whole, which is shorter than its diff:
```python
import jax
import jax.numpy as jnp
from jax import lax
from jax.sharding import PartitionSpec as P

eps_value = 1e-06


def normalize(tokens, gain):
    values = tokens.astype(jnp.float32)
    meansq = jnp.mean(values * values, axis=-1, keepdims=True)
    return (values * lax.rsqrt(meansq + eps_value) * gain).astype(jnp.bfloat16)


def gate_dense(expert_ids, gate_values, number):
    labels = jnp.arange(number, dtype=jnp.int32)
    hits = (expert_ids[..., None] == labels).astype(jnp.float32)
    return jnp.sum(hits * gate_values[..., None], axis=-2)


def dispatch_table(column, capacity):
    matched = (column > 0).astype(jnp.float32)
    slots = jnp.cumsum(matched, axis=-1) - 1.0
    places = jnp.arange(capacity).astype(jnp.float32)
    chosen = (slots[..., None, :] == places[:, None]) & (matched[..., None, :] > 0)
    return chosen


def expert_mlp(slot_rows, gate_matrix, up_matrix, down_matrix):
    gated = jnp.dot(slot_rows, gate_matrix, preferred_element_type=jnp.float32)
    upward = jnp.dot(slot_rows, up_matrix, preferred_element_type=jnp.float32)
    hidden = (jax.nn.silu(gated) * upward).astype(jnp.bfloat16)
    return jnp.dot(hidden, down_matrix, preferred_element_type=jnp.float32).astype(jnp.bfloat16)


def bf16_parts(values, count):
    parts = []
    rest = values
    for _ in range(count):
        head = lax.reduce_precision(rest, exponent_bits=8, mantissa_bits=7)
        parts.append(head.astype(jnp.bfloat16))
        rest = rest - head
    return parts


def local(tokens, gain, expert_ids, gate_values, w_gate, w_up, w_down):
    group = lax.axis_size("expert")
    local_rows, width = tokens.shape
    chosen_count = expert_ids.shape[1]
    number = group * w_gate.shape[0]
    capacity = local_rows * chosen_count // number * 3 // 2
    normed = normalize(tokens, gain)
    dense = gate_dense(expert_ids, gate_values, number)
    column = dense.T
    chosen = dispatch_table(column, capacity)
    table = chosen.astype(jnp.bfloat16)
    send = jnp.einsum("est,td->esd", table, normed, preferred_element_type=jnp.float32)
    send = send.astype(jnp.bfloat16)
    recv = lax.all_to_all(send, "expert", 0, 0, tiled=True)
    outputs = expert_mlp(recv.reshape(-1, width), w_gate[0], w_up[0], w_down[0])
    back = lax.all_to_all(outputs.reshape(group, -1, width), "expert", 0, 0, tiled=True)
    weights = jnp.where(chosen, column[:, None, :], 0.0)
    weights = weights.reshape(-1, local_rows)
    flat = back.reshape(-1, width)
    mixed = None
    for part in bf16_parts(weights, 3):
        term = lax.dot_general(
            part, flat, (((0,), (0,)), ((), ())), preferred_element_type=jnp.float32
        )
        mixed = term if mixed is None else mixed + term
    return mixed.astype(jnp.bfloat16)


def solution(mesh):
    return jax.shard_map(
        local,
        mesh=mesh,
        in_specs=(
            P(("dp", "expert"), None),
            P(),
            P(("dp", "expert"), None),
            P(("dp", "expert"), None),
            P("expert", None, None),
            P("expert", None, None),
            P("expert", None, None),
        ),
        out_specs=P(("dp", "expert"), None),
        check_vma=False,
    )
```

time: 605 us -> 326 us (0.54)
  waiting for transfers between devices: 452 us -> 0 us
  blocking collectives: 44.7 us -> 299 us
  local copies, waits for them, and re-layouts: 31.7 us -> 0.01 us
  matrix products: 55 us -> 23.6 us
  between operations: 13.5 us -> 0.07 us
    all_to_all x0 -> x2, blocking collectives: none -> 299 us  [the longest x1 154 us: local(): recv = lax.all_to_all(send, 'expert', 0, 0, tiled=True)]
    ppermute x15 -> x0, waiting for transfers between devices: 228 us -> none  [passed_along(): return lax.ppermute(block, axis, route)]
    reduce_scatter x1 -> x0, waiting for transfers between devices: 224 us -> none  [local(): lax.psum_scatter((back * column[:, :, None]).reshape(spanned * local_rows...]
    all_gather x1 -> x0, blocking collectives: 44.7 us -> none  [local(): gathered = lax.all_gather(dense, 'expert', axis=0, tiled=True)]
    dot_general x17 -> x4, matrix products: 35.9 us -> 7.35 us  [the longest x3 4.45 us: local(): lax.dot_general(part, flat, (((0,), (0,)), ((), ())), preferred_element_t...]
    while x15 -> x0, local copies, waits for them, and re-layouts: 28.2 us -> none
  transfers between devices with their start and end apart: 16 -> 0, of which waited for: 16 -> 0; matrix products, arithmetic and copies ran while one was open for 0% -> 0% of each run, Pallas kernels for 0% -> 0%
where the time goes in v1:
time: 326 us; the launch traced here: 325 us
  blocking collectives  299 us (92%)
  matrix products  23.6 us (7%)
    all_to_all x1, blocking collectives, local(): recv = lax.all_to_all(send, 'expert', 0, 0, tiled=True)  154 us
    all_to_all x1, blocking collectives, local(): lax.all_to_all(outputs.reshape(group, -1, width), 'expert', 0, 0, tiled=T...  146 us

profile of v1, /device:TPU:2, one launch (start us, length us, event | category | flops | bytes accessed | tf_op | source)
XLA Modules:
  0.0 325.4 jit_solution(16814126012937938397)
XLA Ops:
  0.0 0.0 copy-start
  0.0 1.4 fusion.7
  1.4 0.7 select_reduce_fusion
  2.1 0.3 reduce_window_sum.11
  2.4 2.9 convolution_convert_fusion.1
  5.3 0.0 copy-start.1
  5.3 153.7 %all_to_all.10 = bf16[16,96,2048]{2,1,0:T(8,128)(2,1)S(1)} all-to-all(bf16[16,96,2048]{2,1,0:T(8,128)(2,1)S(1)} %convolution_convert_fusion.1), channel_id=1, replica_groups=mesh['dp'=16,'expert'=16] {'expert'}, dimensions={0} | all-to-all | bytes 12582912 | tf_op jit(solution)/shard_map/all_to_all | solution.py:59
  159.0 0.0 copy-done.1
  159.0 0.0 copy-start.2
  159.0 5.2 %fusion.2 = f32[1536,768]{1,0:T(8,128)S(1)} fusion(bf16[1536,2048]{1,0:T(8,128)(2,1)S(1)} %bitcast.36, bf16[1,2048,768]{2,1,0:T(8,128)(2,1)S(1)} %copy-done.1), kind=kOutput, calls=%fused_computation.5 | convolution fusion | flops 4831838208 | bytes 14155776 | tf_op jit(solution)/shard_map/dot_general | solution.py:30
  164.2 0.0 copy-done.2
  164.2 5.6 %multiply_convert_fusion = bf16[1536,768]{1,0:T(8,128)(2,1)S(1)} fusion(f32[1536,768]{1,0:T(8,128)S(1)} %fusion.2, bf16[1536,2048]{1,0:T(8,128)(2,1)S(1)} %bitcast.37, bf16[1,2048,768]{2,1,0:T(8,128)(2,1)S(1)} %copy-done.2), kind=kOutput, calls=%fused_computation.1 | convolution fusion | flops 4838916096 | bytes 16515072 | tf_op jit(solution)/shard_map/dot_general | solution.py:31
  169.9 0.0 copy-done
  169.9 5.4 %convolution_convert_fusion = bf16[1536,2048]{1,0:T(8,128)(2,1)S(1)} fusion(bf16[1536,768]{1,0:T(8,128)(2,1)S(1)} %multiply_convert_fusion, bf16[1,768,2048]{2,1,0:T(8,128)(2,1)S(1)} %copy-done), kind=kOutput, calls=%fused_computation | convolution fusion | flops 4834983936 | bytes 11796480 | tf_op jit(solution)/shard_map/dot_general | solution.py:33
  175.3 145.7 %all_to_all.11 = bf16[16,96,2048]{2,1,0:T(8,128)(2,1)S(1)} all-to-all(bf16[16,96,2048]{2,1,0:T(8,128)(2,1)S(1)} %bitcast.38), channel_id=1, replica_groups=mesh['dp'=16,'expert'=16] {'expert'}, dimensions={0} | all-to-all | bytes 12582912 | tf_op jit(solution)/shard_map/all_to_all | solution.py:61
  320.9 1.3 convolution_bitcast_fusion
  322.2 1.2 convolution_bitcast_fusion.1
  323.4 2.0 fusion.6
  (4 shorter events, 0.0 us)
Async XLA Ops:
  0.0 169.9 %copy-start = (bf16[1,768,2048]{2,1,0:T(8,128)(2,1)S(1)}, bf16[1,768,2048]{2,1,0:T(8,128)(2,1)}, u32[]{:S(2)}) copy-start(bf16[1,768,2048]{2,1,0:T(8,128)(2,1)} %param.13) | copy-start | bytes 9437188
  5.3 153.7 %copy-start.1 = (bf16[1,2048,768]{2,1,0:T(8,128)(2,1)S(1)}, bf16[1,2048,768]{2,1,0:T(8,128)(2,1)}, u32[]{:S(2)}) copy-start(bf16[1,2048,768]{2,1,0:T(8,128)(2,1)} %param.11) | copy-start | bytes 9437188
  159.0 5.2 %copy-start.2 = (bf16[1,2048,768]{2,1,0:T(8,128)(2,1)S(1)}, bf16[1,2048,768]{2,1,0:T(8,128)(2,1)}, u32[]{:S(2)}) copy-start(bf16[1,2048,768]{2,1,0:T(8,128)(2,1)} %param.12) | copy-start | bytes 9437188
